TPU v7x, 512 devices: a whole 4x4x16 slice. The times are simulated.
512 devices in a mesh: band: 16 (over y, x), pix: 32 (over z, core).
Axes of the slice: x: 4, y: 4, z: 16, core: 2. Of those that a mesh axis runs over, the one named last changes fastest.
Arguments:
- pixels: bfloat16 [512, 32, 1024], P('pix', 'band'), may hold values from -6 to 6
- clear_count: int32 [32], P('pix'), may hold values from 3 to 10, as said below
- clear_index: int32 [320], P('pix'), may hold values from 0 to 15, as said below
- attn_gain: float32 [1024], replicated, may hold values from 0.1 to 1.9
- w_query: bfloat16 [1024, 1024], P(None, 'band')
- w_key: bfloat16 [1024, 1024], P(None, 'band')
- w_value: bfloat16 [1024, 1024], P(None, 'band'), may hold values from -0.1875 to 0.1875
- w_out: bfloat16 [1024, 1024], P('band'), may hold values from -0.1875 to 0.1875
- mlp_gain: float32 [1024], replicated, may hold values from 0.1 to 1.9
- w_gate: bfloat16 [1024, 4096], P(None, 'band'), may hold values from -0.1875 to 0.1875
- w_up: bfloat16 [1024, 4096], P(None, 'band'), may hold values from -0.1875 to 0.1875
- w_down: bfloat16 [4096, 1024], P('band'), may hold values from -0.09375 to 0.09375
Outputs:
- updated: bfloat16 [512, 32, 1024], P('pix', 'band')
Inputs may be any that keep to these rules, and one draw needn't show every extreme that they name: `clear_count`: some tile, drawn from the seed, keeps exactly 10 clear pixels. `clear_index`: for tile t, entries t*10 to t*10+clear_count[t]-1 are distinct local pixel indices in rising order; the tile's remaining entries are 0.
All inputs are finite; a program needn't handle non-finite values.
Results may differ from a plain program's by a relative error of at most 0.019.
Values may be sent and summed in bfloat16 or wider, within the bound.
No kernel may reach another device: no remote copies, remote signals or barrier semaphores. Data moves between devices by JAX's collectives and lax.ppermute only.
A program may use at most 64 MiB of HBM per device.

v0:
```python
import jax
import jax.numpy as jnp
from jax import lax
from jax.sharding import PartitionSpec as P

HD = 64


def normed(rows, gain):
    full = rows.astype(jnp.float32)
    scaled = full * lax.rsqrt(jnp.mean(full * full, axis=-1, keepdims=True) + 1e-05)
    return (scaled * gain).astype(jnp.bfloat16)


def slot_live(number, slots_per_tile, counts):
    slot = jnp.arange(number, dtype=jnp.int32)
    owner = slot // slots_per_tile
    owned = owner[:, None] == jnp.arange(counts.shape[0], dtype=jnp.int32)[None, :]
    owner_count = jnp.sum(jnp.where(owned, counts[None, :], 0), axis=1)
    return slot % slots_per_tile < owner_count


def shards(
    pixels,
    clear_count,
    clear_index,
    attn_gain,
    w_query,
    w_key,
    w_value,
    w_out,
    mlp_gain,
    w_gate,
    w_up,
    w_down,
):
    own_count = clear_count[0]
    kept = jnp.take(pixels, clear_index, axis=0)
    kept_rows = jnp.swapaxes(kept, 0, 1)
    all_rows = lax.all_gather(kept_rows, "band", axis=0, tiled=True)
    spec, slots_here, width = all_rows.shape
    heads_here = w_query.shape[1] // HD
    flat = normed(all_rows, attn_gain).reshape(spec * slots_here, width)

    def project(weight):
        out = jnp.dot(flat, weight, preferred_element_type=jnp.float32).astype(jnp.bfloat16)
        return out.reshape(spec, slots_here, heads_here, HD)

    query = project(w_query)
    key = project(w_key)
    value = project(w_value)
    counts = lax.all_gather(clear_count, "pix", axis=0, tiled=True)
    start_top = jnp.full((spec, heads_here, slots_here), -1e30, jnp.float32)
    top = start_top
    key_piece = lax.all_gather(key, "pix", axis=1, tiled=True)
    value_piece = lax.all_gather(value, "pix", axis=1, tiled=True)
    live = slot_live(key_piece.shape[1], slots_here, counts)
    scores = jnp.einsum(
        "sqhd,skhd->shqk", query, key_piece, preferred_element_type=jnp.float32
    ) * HD ** (-0.5)
    masked = jnp.where(live[None, None, None, :], scores, -1e30)
    new_top = jnp.maximum(top, jnp.max(masked, axis=-1))
    expo = jnp.where(live[None, None, None, :], jnp.exp(masked - new_top[..., None]), 0.0)
    totals = jnp.sum(expo, axis=-1)
    mixed = jnp.einsum(
        "shqk,skhd->sqhd",
        expo.astype(jnp.bfloat16),
        value_piece,
        preferred_element_type=jnp.float32,
    )
    acc = mixed
    top, totals, acc = (new_top, totals, acc)
    context = (acc / jnp.transpose(totals, (0, 2, 1))[..., None]).astype(jnp.bfloat16)
    context_rows = context.reshape(spec, slots_here, heads_here * HD)
    spec_here = spec // lax.axis_size("band")
    piece = context_rows
    out = jnp.dot(
        piece.reshape(spec_here * lax.axis_size("band") * slots_here, heads_here * HD),
        w_out,
        preferred_element_type=jnp.float32,
    )
    attn_out = lax.psum_scatter(
        out.reshape(spec_here * lax.axis_size("band"), slots_here, width).astype(jnp.bfloat16),
        "band",
        scatter_dimension=0,
        tiled=True,
    ).astype(jnp.float32)
    state = (kept_rows.astype(jnp.float32) + attn_out).astype(jnp.bfloat16)
    mlp_in = lax.all_gather(normed(state, mlp_gain), "band", axis=0, tiled=True)
    piece = mlp_in.reshape(spec_here * lax.axis_size("band") * slots_here, width)
    gate = jnp.dot(piece, w_gate, preferred_element_type=jnp.float32)
    upper = jnp.dot(piece, w_up, preferred_element_type=jnp.float32)
    hidden = (jax.nn.silu(gate) * upper).astype(jnp.bfloat16)
    out = jnp.dot(hidden, w_down, preferred_element_type=jnp.float32)
    mlp_out = lax.psum_scatter(
        out.reshape(spec_here * lax.axis_size("band"), slots_here, width).astype(jnp.bfloat16),
        "band",
        scatter_dimension=0,
        tiled=True,
    ).astype(jnp.float32)
    encoded = (state.astype(jnp.float32) + mlp_out).astype(jnp.bfloat16)
    live_here = jnp.arange(slots_here, dtype=jnp.int32) < own_count
    chosen = (
        jnp.arange(pixels.shape[0], dtype=jnp.int32)[:, None] == clear_index[None, :]
    ) & live_here[None, :]
    placed = jnp.einsum(
        "pc,scd->psd", chosen.astype(jnp.bfloat16), encoded, preferred_element_type=jnp.float32
    ).astype(jnp.bfloat16)
    taken = jnp.any(chosen, axis=1)
    return jnp.where(taken[:, None, None], placed, pixels)


def solution(mesh):
    return jax.shard_map(
        shards,
        mesh=mesh,
        in_specs=(
            P("pix", "band", None),
            P("pix"),
            P("pix"),
            P(),
            P(None, "band"),
            P(None, "band"),
            P(None, "band"),
            P("band", None),
            P(),
            P(None, "band"),
            P(None, "band"),
            P("band", None),
        ),
        out_specs=P("pix", "band", None),
        check_vma=False,
    )
```

profile of v0, /device:TPU:2, one launch (start us, length us, event | category | flops | bytes accessed | tf_op | source)
XLA Modules:
  0.0 454.2 jit_solution(5196698798898972980)
XLA Ops:
  6.5 0.7 compare_select_fusion
  7.3 0.7 compare_and_fusion
  7.9 1.5 gather_fusion
  9.4 0.1 fusion.46
  9.6 27.7 %all_gather.15 = bf16[32,10,1024]{2,1,0:T(8,128)(2,1)S(1)} all-gather(bf16[2,10,1024]{2,1,0:T(8,128)(2,1)S(1)} %copy.59), channel_id=1, replica_groups=mesh['band'=16,'pix'=32] {'band'}, dimensions={0}, use_global_device_ids=true | all-gather | bytes 696320 | tf_op jit(solution)/shard_map/all_gather | solution.py:40
  37.3 0.3 fusion
  37.6 0.3 fusion.2
  37.9 0.2 reshape.109
  38.2 0.3 copy-done.2
  38.5 0.3 convolution_convert_fusion.3
  38.9 0.1 copy.64
  39.0 0.7 copy.65
  39.7 0.0 all-gather.3.cloned.1.call-start
  39.8 0.3 convolution_convert_fusion.5
  40.1 0.1 copy.60
  40.3 0.7 copy.61
  41.0 0.0 all-reduce.6.cloned.1.call-start
  41.1 0.3 convolution_convert_fusion.4
  41.4 0.1 copy.63
  42.2 1.3 dynamic-slice
  43.5 0.7 dynamic-update-slice
  44.2 24.1 %all-reduce = s32[32]{0:T(128)S(1)} all-reduce(s32[32]{0:T(128)S(1)} %dynamic-update-slice), channel_id=1, replica_groups=mesh['band'=16,'pix'=32] {'pix'}, use_global_device_ids=true, to_apply=%add | all-reduce | flops 32 | bytes 256
  68.3 0.1 select_reduce_fusion
  68.4 43.2 %all-gather.5.cloned.1.call-done = bf16[32,320,1,64]{3,0,2,1:T(8,128)(2,1)} async-done(((bf16[32,10,1,64]{3,0,2,1:T(8,128)(2,1)}), bf16[32,320,1,64]{3,0,2,1:T(8,128)(2,1)}) %all-gather.5.cloned.1.call-update) | async-done | bytes 1310736 | tf_op jit(solution)/shard_map/all_gather | solution.py:55
  111.6 4.4 copy.66
  116.0 0.5 fusion.61
  116.5 0.3 fusion.27
  116.8 65.8 %all-gather.3.cloned.1.call-done = bf16[32,320,1,64]{3,0,2,1:T(8,128)(2,1)} async-done(((bf16[32,10,1,64]{3,0,2,1:T(8,128)(2,1)}), bf16[32,320,1,64]{3,0,2,1:T(8,128)(2,1)}) %all-gather.3.cloned.1.call-update) | async-done | bytes 1310736 | tf_op jit(solution)/shard_map/all_gather | solution.py:56
  182.7 4.4 copy.62
  187.1 0.7 fusion.24
  187.8 0.2 copy-done.5
  188.0 1.2 convolution_convert_fusion
  189.3 1.3 dynamic-slice.1
  191.2 110.8 %all-reduce.6.cloned.1.call-done = bf16[32,10,1024]{2,0,1:T(8,128)(2,1)} async-done(((bf16[32,10,1024]{2,0,1:T(8,128)(2,1)}), bf16[32,10,1024]{2,0,1:T(8,128)(2,1)}) %all-reduce.6.cloned.1.call-update) | async-done | bytes 655376
  302.0 1.1 fusion.40
  303.2 0.1 fusion.42
  303.3 23.2 %all_gather.19 = bf16[32,10,1024]{2,1,0:T(8,128)(2,1)S(1)} all-gather(bf16[2,10,1024]{2,1,0:T(8,128)(2,1)S(1)} %copy.68), channel_id=1, replica_groups=mesh['band'=16,'pix'=32] {'band'}, dimensions={0}, use_global_device_ids=true | all-gather | bytes 696320 | tf_op jit(solution)/shard_map/all_gather | solution.py:89
  326.5 0.2 reshape.115
  326.8 0.3 fusion.62
  327.1 0.4 copy-done.9
  327.6 0.9 convolution_convert_fusion.1
  328.4 0.2 convert_element_type.79
  328.7 1.2 copy.69
  329.9 0.1 fusion.49
  330.0 115.7 %all-reduce.8.cloned.1.call-done = bf16[32,10,1024]{2,0,1:T(8,128)(2,1)} async-done(((bf16[32,10,1024]{2,0,1:T(8,128)(2,1)}), bf16[32,10,1024]{2,0,1:T(8,128)(2,1)}) %all-reduce.8.cloned.1.call-update) | async-done | bytes 655376
  445.8 1.0 fusion.43
  446.8 0.1 fusion.17
  446.9 0.7 copy.72
  (38 shorter events, 0.4 us)
Async XLA Ops:
  6.5 320.6 %copy-start = (bf16[256,1024]{1,0:T(8,128)(2,1)S(1)}, bf16[256,1024]{1,0:T(8,128)(2,1)}, u32[]{:S(2)}) copy-start(bf16[256,1024]{1,0:T(8,128)(2,1)} %param.23) | copy-start | bytes 1572868
  6.5 31.1 %copy-start.7 = (f32[1024]{0:T(1024)S(1)}, f32[1024]{0:T(1024)}, u32[]{:S(2)}) copy-start(f32[1024]{0:T(1024)} %param.15) | copy-start | bytes 12292
  6.5 105.1 %all-gather.5.cloned.1.call-start = ((), (), s32[]{:S(2)}) async-start(), calls=%async_computation.1 | async-start | bytes 2703360 | tf_op jit(solution)/shard_map/all_gather | solution.py:55
  37.6 0.9 copy-start.2
  37.9 1.8 copy-start.3
  38.5 2.5 copy-start.4
  39.7 142.9 %all-gather.3.cloned.1.call-start = ((), (), s32[]{:S(2)}) async-start(), calls=%async_computation | async-start | bytes 2703360 | tf_op jit(solution)/shard_map/all_gather | solution.py:56
  41.0 261.0 %all-reduce.6.cloned.1.call-start = ((), (), s32[]{:S(2)}) async-start(), calls=%async_computation.2 | async-start | bytes 1310720
  187.1 0.9 copy-start.5
  188.0 115.2 %copy-start.8 = (f32[1024]{0:T(1024)S(1)}, f32[1024]{0:T(1024)}, u32[]{:S(2)}) copy-start(f32[1024]{0:T(1024)} %param.20) | copy-start | bytes 12292
  189.2 256.6 %all-reduce.8.cloned.1.call-start = ((), (), s32[]{:S(2)}) async-start(), calls=%async_computation.3 | async-start | bytes 1310720
  191.2 135.5 %copy-start.1 = (bf16[1024,256]{1,0:T(8,128)(2,1)S(1)}, bf16[1024,256]{1,0:T(8,128)(2,1)}, u32[]{:S(2)}) copy-start(bf16[1024,256]{1,0:T(8,128)(2,1)} %param.21) | copy-start | bytes 1572868
  326.5 1.0 copy-start.9
  328.6 1.3 copy-start.10
  328.6 118.1 %copy-start.6 = (bf16[16,2,1024]{2,1,0:T(2,128)(2,1)S(1)}, bf16[16,2,1024]{2,1,0:T(2,128)(2,1)}, u32[]{:S(2)}) copy-start(bf16[16,2,1024]{2,1,0:T(2,128)(2,1)} %param.12) | copy-start | bytes 196612
Sparse Core Ops, SparseCore 0:
  39.8 71.7 all-gather.4
  113.7 68.9 all-gather.2
  189.3 112.6 all-reduce.5
  330.0 115.7 all-reduce.7
where the time goes:
time: 455 us; the launch traced here: 454 us
  waiting for transfers between devices  336 us (74%)
  blocking collectives  75 us (16%)
  local copies, waits for them, and re-layouts  19 us (4%)
  between operations  14.7 us (3%)
  other arithmetic  4.92 us (1%)
  matrix products  4.72 us (1%)
    unnamed x6, waiting for transfers between devices  227 us
    all_gather x1, waiting for transfers between devices, shards(): value_piece = lax.all_gather(value, 'pix', axis=1, tiled=True)  65.8 us
    all_gather x1, waiting for transfers between devices, shards(): key_piece = lax.all_gather(key, 'pix', axis=1, tiled=True)  43.2 us
    all_gather x1, blocking collectives, shards(): all_rows = lax.all_gather(kept_rows, 'band', axis=0, tiled=True)  27.7 us
    unnamed x1, blocking collectives  24.1 us
    all_gather x1, blocking collectives, shards(): mlp_in = lax.all_gather(normed(state, mlp_gain), 'band', axis=0, tiled=True)  23.2 us
  transfers between devices with their start and end apart: 4, of which 4 were waited for; matrix products, arithmetic and copies ran while one was open for 2% of the time, Pallas kernels for 0%

commit v1 on v0

--- a/solution.py
+++ b/solution.py
@@ -86,7 +86,25 @@
         tiled=True,
     ).astype(jnp.float32)
     state = (kept_rows.astype(jnp.float32) + attn_out).astype(jnp.bfloat16)
-    mlp_in = lax.all_gather(normed(state, mlp_gain), "band", axis=0, tiled=True)
+    array = normed(state, mlp_gain)
+    ways, here, step = (lax.axis_size("band"), lax.axis_index("band"), array.shape[0])
+    lengths = [n * ways if d == 0 else n for d, n in enumerate(array.shape)]
+    mlp_in = lax.dynamic_update_slice_in_dim(
+        jnp.zeros(lengths, array.dtype), array, here * step, axis=0
+    )
+    going_up = going_down = array
+    for far in range(1, ways // 2 + 1):
+        going_up = lax.ppermute(going_up, "band", [(d, (d + 1) % ways) for d in range(ways)])
+        mlp_in = lax.dynamic_update_slice_in_dim(
+            mlp_in, going_up, (here - far) % ways * step, axis=0
+        )
+        if 2 * far < ways:
+            going_down = lax.ppermute(
+                going_down, "band", [(d, (d - 1) % ways) for d in range(ways)]
+            )
+            mlp_in = lax.dynamic_update_slice_in_dim(
+                mlp_in, going_down, (here + far) % ways * step, axis=0
+            )
     piece = mlp_in.reshape(spec_here * lax.axis_size("band") * slots_here, width)
     gate = jnp.dot(piece, w_gate, preferred_element_type=jnp.float32)
     upper = jnp.dot(piece, w_up, preferred_element_type=jnp.float32)

time: 455 us -> 503 us (1.11)
  starting transfers between devices: 0.13 us -> 61.9 us
  blocking collectives: 75 us -> 51.9 us
  waiting for transfers between devices: 336 us -> 344 us
    ppermute x0 -> x15, starting transfers between devices: none -> 61.7 us  [the longest x7 44.6 us: shards(): lax.ppermute(going_down, 'band', [(d, (d - 1) % ways) for d in range(ways)])]
    all_gather x1 -> x0, blocking collectives: 23.2 us -> none  [shards(): mlp_in = lax.all_gather(normed(state, mlp_gain), 'band', axis=0, tiled=True)]
    ppermute x0 -> x15, waiting for transfers between devices: none -> 7.27 us  [the longest x8 7.25 us: shards(): lax.ppermute(going_up, 'band', [(d, (d + 1) % ways) for d in range(ways)])]
  transfers between devices with their start and end apart: 4 -> 19, of which waited for: 4 -> 5; matrix products, arithmetic and copies ran while one was open for 2% -> 2% of each run, Pallas kernels for 0% -> 0%
where the time goes in v1:
time: 503 us
  waiting for transfers between devices  344 us (68%)
  starting transfers between devices  61.9 us (12%)
  blocking collectives  51.9 us (10%)
  local copies, waits for them, and re-layouts  19 us (4%)
  between operations  15.4 us (3%)
  matrix products  5.77 us (1%)
    unnamed x6, waiting for transfers between devices  228 us
    all_gather x1, waiting for transfers between devices, shards(): value_piece = lax.all_gather(value, 'pix', axis=1, tiled=True)  65.8 us
    ppermute x7, starting transfers between devices, shards(): lax.ppermute(going_down, 'band', [(d, (d - 1) % ways) for d in range(ways)])  44.6 us
    all_gather x1, waiting for transfers between devices, shards(): key_piece = lax.all_gather(key, 'pix', axis=1, tiled=True)  43 us
    all_gather x1, blocking collectives, shards(): all_rows = lax.all_gather(kept_rows, 'band', axis=0, tiled=True)  27.7 us
    unnamed x1, blocking collectives  24.2 us
    ppermute x8, starting transfers between devices, shards(): lax.ppermute(going_up, 'band', [(d, (d + 1) % ways) for d in range(ways)])  17.1 us
  transfers between devices with their start and end apart: 19, of which 5 were waited for; matrix products, arithmetic and copies ran while one was open for 2% of the time, Pallas kernels for 0%

profile of v1, /device:TPU:2, one launch (start us, length us, event | category | flops | bytes accessed | tf_op | source)
XLA Modules:
  0.0 502.6 jit_solution(18332661027966979130)
XLA Ops:
  6.5 0.7 compare_select_fusion
  7.3 0.7 compare_and_fusion
  7.9 1.5 gather_fusion
  9.6 27.7 %all_gather.12 = bf16[32,10,1024]{2,1,0:T(8,128)(2,1)S(1)} all-gather(bf16[2,10,1024]{2,1,0:T(8,128)(2,1)S(1)} %copy.89), channel_id=1, replica_groups=mesh['band'=16,'pix'=32] {'band'}, dimensions={0}, use_global_device_ids=true | all-gather | bytes 696320 | tf_op jit(solution)/shard_map/all_gather | solution.py:40
  37.3 0.3 fusion
  37.6 0.3 fusion.2
  38.2 0.3 copy-done.2
  38.5 0.3 convolution_convert_fusion.3
  39.0 0.7 copy.95
  39.8 0.3 convolution_convert_fusion.5
  40.3 0.7 copy.91
  41.1 0.3 convolution_convert_fusion.4
  42.2 1.3 dynamic-slice
  43.5 0.7 dynamic-update-slice
  44.3 24.2 %all-reduce = s32[32]{0:T(128)S(1)} all-reduce(s32[32]{0:T(128)S(1)} %dynamic-update-slice), channel_id=1, replica_groups=mesh['band'=16,'pix'=32] {'pix'}, use_global_device_ids=true, to_apply=%add | all-reduce | flops 32 | bytes 256
  68.5 43.0 %all-gather.5.cloned.1.call-done = bf16[32,320,1,64]{3,0,2,1:T(8,128)(2,1)} async-done(((bf16[32,10,1,64]{3,0,2,1:T(8,128)(2,1)}), bf16[32,320,1,64]{3,0,2,1:T(8,128)(2,1)}) %all-gather.5.cloned.1.call-update) | async-done | bytes 1310736 | tf_op jit(solution)/shard_map/all_gather | solution.py:55
  111.6 4.4 copy.96
  116.0 0.5 fusion.55
  116.5 0.3 fusion.26
  116.8 65.8 %all-gather.3.cloned.1.call-done = bf16[32,320,1,64]{3,0,2,1:T(8,128)(2,1)} async-done(((bf16[32,10,1,64]{3,0,2,1:T(8,128)(2,1)}), bf16[32,320,1,64]{3,0,2,1:T(8,128)(2,1)}) %all-gather.3.cloned.1.call-update) | async-done | bytes 1310736 | tf_op jit(solution)/shard_map/all_gather | solution.py:56
  182.6 4.4 copy.92
  187.1 0.7 fusion.23
  188.0 1.2 convolution_convert_fusion
  189.5 1.3 dynamic-slice.1
  191.5 110.5 %all-reduce.6.cloned.1.call-done = bf16[32,10,1024]{2,0,1:T(8,128)(2,1)} async-done(((bf16[32,10,1024]{2,0,1:T(8,128)(2,1)}), bf16[32,10,1024]{2,0,1:T(8,128)(2,1)}) %all-reduce.6.cloned.1.call-update) | async-done | bytes 655376
  302.0 1.1 fusion.34
  303.3 2.7 collective-permute-start
  306.0 3.1 collective-permute-start.1
  309.3 2.7 collective-permute-start.2
  312.0 5.3 %collective-permute-start.3 = (bf16[2,10,1024]{2,0,1:T(2,128)(2,1)S(1)}, bf16[2,10,1024]{2,0,1:T(2,128)(2,1)S(1)}, u32[]{:S(2)}, u32[]{:S(2)}) collective-permute-start(bf16[2,10,1024]{2,0,1:T(2,128)(2,1)S(1)} %collective-permute-done.1), channel_id=1, source_target_pairs={{0,480},{32,0},{64,32},{96,64},{128,96},{160,128},{192,160},{224,1... | collective-permute-start | bytes 122888 | tf_op jit(solution)/shard_map/ppermute | solution.py:102
  317.4 2.1 collective-permute-start.4
  319.5 7.2 %collective-permute-start.5 = (bf16[2,10,1024]{2,0,1:T(2,128)(2,1)S(1)}, bf16[2,10,1024]{2,0,1:T(2,128)(2,1)S(1)}, u32[]{:S(2)}, u32[]{:S(2)}) collective-permute-start(bf16[2,10,1024]{2,0,1:T(2,128)(2,1)S(1)} %collective-permute-done.3), channel_id=1, source_target_pairs={{0,480},{32,0},{64,32},{96,64},{128,96},{160,128},{192,160},{224,1... | collective-permute-start | bytes 122888 | tf_op jit(solution)/shard_map/ppermute | solution.py:102
  326.8 1.9 collective-permute-start.6
  328.7 7.2 %collective-permute-start.7 = (bf16[2,10,1024]{2,0,1:T(2,128)(2,1)S(1)}, bf16[2,10,1024]{2,0,1:T(2,128)(2,1)S(1)}, u32[]{:S(2)}, u32[]{:S(2)}) collective-permute-start(bf16[2,10,1024]{2,0,1:T(2,128)(2,1)S(1)} %collective-permute-done.5), channel_id=1, source_target_pairs={{0,480},{32,0},{64,32},{96,64},{128,96},{160,128},{192,160},{224,1... | collective-permute-start | bytes 122888 | tf_op jit(solution)/shard_map/ppermute | solution.py:102
  336.0 1.9 collective-permute-start.8
  338.0 7.2 %collective-permute-start.9 = (bf16[2,10,1024]{2,0,1:T(2,128)(2,1)S(1)}, bf16[2,10,1024]{2,0,1:T(2,128)(2,1)S(1)}, u32[]{:S(2)}, u32[]{:S(2)}) collective-permute-start(bf16[2,10,1024]{2,0,1:T(2,128)(2,1)S(1)} %collective-permute-done.7), channel_id=1, source_target_pairs={{0,480},{32,0},{64,32},{96,64},{128,96},{160,128},{192,160},{224,1... | collective-permute-start | bytes 122888 | tf_op jit(solution)/shard_map/ppermute | solution.py:102
  345.3 1.9 collective-permute-start.10
  347.2 7.2 %collective-permute-start.11 = (bf16[2,10,1024]{2,0,1:T(2,128)(2,1)S(1)}, bf16[2,10,1024]{2,0,1:T(2,128)(2,1)S(1)}, u32[]{:S(2)}, u32[]{:S(2)}) collective-permute-start(bf16[2,10,1024]{2,0,1:T(2,128)(2,1)S(1)} %collective-permute-done.9), channel_id=1, source_target_pairs={{0,480},{32,0},{64,32},{96,64},{128,96},{160,128},{192,160},{224,1... | collective-permute-start | bytes 122888 | tf_op jit(solution)/shard_map/ppermute | solution.py:102
  354.5 1.9 collective-permute-start.12
  356.5 7.2 %collective-permute-start.13 = (bf16[2,10,1024]{2,0,1:T(2,128)(2,1)S(1)}, bf16[2,10,1024]{2,0,1:T(2,128)(2,1)S(1)}, u32[]{:S(2)}, u32[]{:S(2)}) collective-permute-start(bf16[2,10,1024]{2,0,1:T(2,128)(2,1)S(1)} %collective-permute-done.11), channel_id=1, source_target_pairs={{0,480},{32,0},{64,32},{96,64},{128,96},{160,128},{192,160},{224,1... | collective-permute-start | bytes 122888 | tf_op jit(solution)/shard_map/ppermute | solution.py:102
  363.8 1.9 collective-permute-start.14
  365.8 7.2 %collective-permute-done.14 = bf16[2,10,1024]{2,0,1:T(2,128)(2,1)S(1)} collective-permute-done((bf16[2,10,1024]{2,0,1:T(2,128)(2,1)S(1)}, bf16[2,10,1024]{2,0,1:T(2,128)(2,1)S(1)}, u32[]{:S(2)}, u32[]{:S(2)}) %collective-permute-start.14) | collective-permute-done | bytes 40992 | tf_op jit(solution)/shard_map/ppermute | solution.py:97
  373.3 0.3 fusion.58
  373.6 1.9 convolution_convert_fusion.1
  375.8 1.2 copy.114
  377.2 117.1 %all-reduce.8.cloned.1.call-done = bf16[32,10,1024]{2,0,1:T(8,128)(2,1)} async-done(((bf16[32,10,1024]{2,0,1:T(8,128)(2,1)}), bf16[32,10,1024]{2,0,1:T(8,128)(2,1)}) %all-reduce.8.cloned.1.call-update) | async-done | bytes 655376
  494.2 1.0 fusion.37
  495.4 0.7 copy.117
  (81 shorter events, 2.6 us)
Async XLA Ops:
  6.5 367.1 %copy-start = (bf16[256,1024]{1,0:T(8,128)(2,1)S(1)}, bf16[256,1024]{1,0:T(8,128)(2,1)}, u32[]{:S(2)}) copy-start(bf16[256,1024]{1,0:T(8,128)(2,1)} %param.23) | copy-start | bytes 1572868
  6.5 31.1 %copy-start.7 = (f32[1024]{0:T(1024)S(1)}, f32[1024]{0:T(1024)}, u32[]{:S(2)}) copy-start(f32[1024]{0:T(1024)} %param.15) | copy-start | bytes 12292
  6.5 105.0 %all-gather.5.cloned.1.call-start = ((), (), s32[]{:S(2)}) async-start(), calls=%async_computation.1 | async-start | bytes 2703360 | tf_op jit(solution)/shard_map/all_gather | solution.py:55
  37.6 0.9 copy-start.2
  37.9 1.9 copy-start.3
  38.5 2.5 copy-start.4
  39.7 142.9 %all-gather.3.cloned.1.call-start = ((), (), s32[]{:S(2)}) async-start(), calls=%async_computation | async-start | bytes 2703360 | tf_op jit(solution)/shard_map/all_gather | solution.py:56
  41.0 261.0 %all-reduce.6.cloned.1.call-start = ((), (), s32[]{:S(2)}) async-start(), calls=%async_computation.2 | async-start | bytes 1310720
  187.1 0.9 copy-start.5
  188.0 115.2 %copy-start.8 = (f32[1024]{0:T(1024)S(1)}, f32[1024]{0:T(1024)}, u32[]{:S(2)}) copy-start(f32[1024]{0:T(1024)} %param.20) | copy-start | bytes 12292
  189.2 305.0 %all-reduce.8.cloned.1.call-start = ((), (), s32[]{:S(2)}) async-start(), calls=%async_computation.3 | async-start | bytes 1310720
  303.3 6.0 %collective-permute-start = (bf16[2,10,1024]{2,0,1:T(2,128)(2,1)S(1)}, bf16[2,10,1024]{2,0,1:T(2,128)(2,1)S(1)}, u32[]{:S(2)}, u32[]{:S(2)}) collective-permute-start(bf16[2,10,1024]{2,0,1:T(2,128)(2,1)S(1)} %fusion.36), channel_id=1, source_target_pairs={{0,32},{32,64},{64,96},{96,128},{128,160},{160,192},{192,224},{224... | collective-permute-start | bytes 122888 | tf_op jit(solution)/shard_map/ppermute | solution.py:97
  306.0 6.0 %collective-permute-start.1 = (bf16[2,10,1024]{2,0,1:T(2,128)(2,1)S(1)}, bf16[2,10,1024]{2,0,1:T(2,128)(2,1)S(1)}, u32[]{:S(2)}, u32[]{:S(2)}) collective-permute-start(bf16[2,10,1024]{2,0,1:T(2,128)(2,1)S(1)} %fusion.36), channel_id=1, source_target_pairs={{0,480},{32,0},{64,32},{96,64},{128,96},{160,128},{192,160},{224,1... | collective-permute-start | bytes 122888 | tf_op jit(solution)/shard_map/ppermute | solution.py:102
  309.3 8.1 %collective-permute-start.2 = (bf16[2,10,1024]{2,0,1:T(2,128)(2,1)S(1)}, bf16[2,10,1024]{2,0,1:T(2,128)(2,1)S(1)}, u32[]{:S(2)}, u32[]{:S(2)}) collective-permute-start(bf16[2,10,1024]{2,0,1:T(2,128)(2,1)S(1)} %collective-permute-done), channel_id=1, source_target_pairs={{0,32},{32,64},{64,96},{96,128},{128,160},{160,192},{192,224},{224... | collective-permute-start | bytes 122888 | tf_op jit(solution)/shard_map/ppermute | solution.py:97
  312.0 7.4 %collective-permute-start.3 = (bf16[2,10,1024]{2,0,1:T(2,128)(2,1)S(1)}, bf16[2,10,1024]{2,0,1:T(2,128)(2,1)S(1)}, u32[]{:S(2)}, u32[]{:S(2)}) collective-permute-start(bf16[2,10,1024]{2,0,1:T(2,128)(2,1)S(1)} %collective-permute-done.1), channel_id=1, source_target_pairs={{0,480},{32,0},{64,32},{96,64},{128,96},{160,128},{192,160},{224,1... | collective-permute-start | bytes 122888 | tf_op jit(solution)/shard_map/ppermute | solution.py:102
  317.4 55.9 %copy-start.1 = (bf16[1024,256]{1,0:T(8,128)(2,1)S(1)}, bf16[1024,256]{1,0:T(8,128)(2,1)}, u32[]{:S(2)}) copy-start(bf16[1024,256]{1,0:T(8,128)(2,1)} %param.21) | copy-start | bytes 1572868
  317.4 9.4 %collective-permute-start.4 = (bf16[2,10,1024]{2,0,1:T(2,128)(2,1)S(1)}, bf16[2,10,1024]{2,0,1:T(2,128)(2,1)S(1)}, u32[]{:S(2)}, u32[]{:S(2)}) collective-permute-start(bf16[2,10,1024]{2,0,1:T(2,128)(2,1)S(1)} %collective-permute-done.2), channel_id=1, source_target_pairs={{0,32},{32,64},{64,96},{96,128},{128,160},{160,192},{192,224},{224... | collective-permute-start | bytes 122888 | tf_op jit(solution)/shard_map/ppermute | solution.py:97
  319.5 9.2 %collective-permute-start.5 = (bf16[2,10,1024]{2,0,1:T(2,128)(2,1)S(1)}, bf16[2,10,1024]{2,0,1:T(2,128)(2,1)S(1)}, u32[]{:S(2)}, u32[]{:S(2)}) collective-permute-start(bf16[2,10,1024]{2,0,1:T(2,128)(2,1)S(1)} %collective-permute-done.3), channel_id=1, source_target_pairs={{0,480},{32,0},{64,32},{96,64},{128,96},{160,128},{192,160},{224,1... | collective-permute-start | bytes 122888 | tf_op jit(solution)/shard_map/ppermute | solution.py:102
  326.8 9.2 %collective-permute-start.6 = (bf16[2,10,1024]{2,0,1:T(2,128)(2,1)S(1)}, bf16[2,10,1024]{2,0,1:T(2,128)(2,1)S(1)}, u32[]{:S(2)}, u32[]{:S(2)}) collective-permute-start(bf16[2,10,1024]{2,0,1:T(2,128)(2,1)S(1)} %collective-permute-done.4), channel_id=1, source_target_pairs={{0,32},{32,64},{64,96},{96,128},{128,160},{160,192},{192,224},{224... | collective-permute-start | bytes 122888 | tf_op jit(solution)/shard_map/ppermute | solution.py:97
  328.7 9.2 %collective-permute-start.7 = (bf16[2,10,1024]{2,0,1:T(2,128)(2,1)S(1)}, bf16[2,10,1024]{2,0,1:T(2,128)(2,1)S(1)}, u32[]{:S(2)}, u32[]{:S(2)}) collective-permute-start(bf16[2,10,1024]{2,0,1:T(2,128)(2,1)S(1)} %collective-permute-done.5), channel_id=1, source_target_pairs={{0,480},{32,0},{64,32},{96,64},{128,96},{160,128},{192,160},{224,1... | collective-permute-start | bytes 122888 | tf_op jit(solution)/shard_map/ppermute | solution.py:102
  336.0 9.2 %collective-permute-start.8 = (bf16[2,10,1024]{2,0,1:T(2,128)(2,1)S(1)}, bf16[2,10,1024]{2,0,1:T(2,128)(2,1)S(1)}, u32[]{:S(2)}, u32[]{:S(2)}) collective-permute-start(bf16[2,10,1024]{2,0,1:T(2,128)(2,1)S(1)} %collective-permute-done.6), channel_id=1, source_target_pairs={{0,32},{32,64},{64,96},{96,128},{128,160},{160,192},{192,224},{224... | collective-permute-start | bytes 122888 | tf_op jit(solution)/shard_map/ppermute | solution.py:97
  338.0 9.2 %collective-permute-start.9 = (bf16[2,10,1024]{2,0,1:T(2,128)(2,1)S(1)}, bf16[2,10,1024]{2,0,1:T(2,128)(2,1)S(1)}, u32[]{:S(2)}, u32[]{:S(2)}) collective-permute-start(bf16[2,10,1024]{2,0,1:T(2,128)(2,1)S(1)} %collective-permute-done.7), channel_id=1, source_target_pairs={{0,480},{32,0},{64,32},{96,64},{128,96},{160,128},{192,160},{224,1... | collective-permute-start | bytes 122888 | tf_op jit(solution)/shard_map/ppermute | solution.py:102
  345.3 9.2 %collective-permute-start.10 = (bf16[2,10,1024]{2,0,1:T(2,128)(2,1)S(1)}, bf16[2,10,1024]{2,0,1:T(2,128)(2,1)S(1)}, u32[]{:S(2)}, u32[]{:S(2)}) collective-permute-start(bf16[2,10,1024]{2,0,1:T(2,128)(2,1)S(1)} %collective-permute-done.8), channel_id=1, source_target_pairs={{0,32},{32,64},{64,96},{96,128},{128,160},{160,192},{192,224},{224... | collective-permute-start | bytes 122888 | tf_op jit(solution)/shard_map/ppermute | solution.py:97
  347.2 9.2 %collective-permute-start.11 = (bf16[2,10,1024]{2,0,1:T(2,128)(2,1)S(1)}, bf16[2,10,1024]{2,0,1:T(2,128)(2,1)S(1)}, u32[]{:S(2)}, u32[]{:S(2)}) collective-permute-start(bf16[2,10,1024]{2,0,1:T(2,128)(2,1)S(1)} %collective-permute-done.9), channel_id=1, source_target_pairs={{0,480},{32,0},{64,32},{96,64},{128,96},{160,128},{192,160},{224,1... | collective-permute-start | bytes 122888 | tf_op jit(solution)/shard_map/ppermute | solution.py:102
  354.5 9.2 %collective-permute-start.12 = (bf16[2,10,1024]{2,0,1:T(2,128)(2,1)S(1)}, bf16[2,10,1024]{2,0,1:T(2,128)(2,1)S(1)}, u32[]{:S(2)}, u32[]{:S(2)}) collective-permute-start(bf16[2,10,1024]{2,0,1:T(2,128)(2,1)S(1)} %collective-permute-done.10), channel_id=1, source_target_pairs={{0,32},{32,64},{64,96},{96,128},{128,160},{160,192},{192,224},{224... | collective-permute-start | bytes 122888 | tf_op jit(solution)/shard_map/ppermute | solution.py:97
  356.5 9.3 %collective-permute-start.13 = (bf16[2,10,1024]{2,0,1:T(2,128)(2,1)S(1)}, bf16[2,10,1024]{2,0,1:T(2,128)(2,1)S(1)}, u32[]{:S(2)}, u32[]{:S(2)}) collective-permute-start(bf16[2,10,1024]{2,0,1:T(2,128)(2,1)S(1)} %collective-permute-done.11), channel_id=1, source_target_pairs={{0,480},{32,0},{64,32},{96,64},{128,96},{160,128},{192,160},{224,1... | collective-permute-start | bytes 122888 | tf_op jit(solution)/shard_map/ppermute | solution.py:102
  363.8 9.2 %collective-permute-start.14 = (bf16[2,10,1024]{2,0,1:T(2,128)(2,1)S(1)}, bf16[2,10,1024]{2,0,1:T(2,128)(2,1)S(1)}, u32[]{:S(2)}, u32[]{:S(2)}) collective-permute-start(bf16[2,10,1024]{2,0,1:T(2,128)(2,1)S(1)} %collective-permute-done.12), channel_id=1, source_target_pairs={{0,32},{32,64},{64,96},{96,128},{128,160},{160,192},{192,224},{224... | collective-permute-start | bytes 122888 | tf_op jit(solution)/shard_map/ppermute | solution.py:97
  375.7 1.3 copy-start.9
  375.8 119.5 %copy-start.6 = (bf16[16,2,1024]{2,1,0:T(2,128)(2,1)S(1)}, bf16[16,2,1024]{2,1,0:T(2,128)(2,1)}, u32[]{:S(2)}) copy-start(bf16[16,2,1024]{2,1,0:T(2,128)(2,1)} %param.12) | copy-start | bytes 196612
Sparse Core Ops, SparseCore 0:
  39.9 71.6 all-gather.4
  113.7 68.9 all-gather.2
  189.3 112.6 all-reduce.5
  377.1 117.0 all-reduce.7
